TPU v7x, 256 devices: a whole 4x4x8 slice. The times are simulated.
256 devices in a mesh: tensor: 32 (over x_hi, z, core), rows: 8 (over x_lo, y).
Axes of the slice: x: 4 (x_hi: 2, x_lo: 2; x = x_hi * 2 + x_lo), y: 4, z: 8, core: 2. Of those that a mesh axis runs over, the one named last changes fastest.
Arguments:
- image: bfloat16 [64, 64, 3072], P('rows', None, 'tensor'), may hold values from -6 to 6
- dw_kernel: bfloat16 [7, 7, 3072], P(None, None, 'tensor'), may hold values from -0.875 to 0.875
- dw_bias: float32 [3072], P('tensor'), may hold values from -3 to 3
- norm_gain: float32 [3072], replicated, may hold values from 0.1 to 1.9
- norm_bias: float32 [3072], replicated, may hold values from -2 to 2
- w_expand: bfloat16 [3072, 12288], P('rows', 'tensor'), may hold values from -0.21875 to 0.21875
- b_expand: float32 [12288], P('tensor'), may hold values from -3 to 3
- w_project: bfloat16 [12288, 3072], P('tensor', 'rows'), may hold values from -0.109375 to 0.109375
- b_project: float32 [3072], P('tensor'), may hold values from -3 to 3
- layer_scale: float32 [3072], P('tensor'), may hold values from 0.25 to 2
- out_grad: bfloat16 [64, 64, 3072], P('rows', None, 'tensor'), may hold values from -6 to 6
Outputs:
- result: bfloat16 [64, 64, 3072], P('rows', None, 'tensor')
- image_grad: bfloat16 [64, 64, 3072], P('rows', None, 'tensor')
- expand_grad: float32 [3072, 12288], P('rows', 'tensor')
- project_grad: float32 [12288, 3072], P('tensor', 'rows')
- kernel_grad: float32 [7, 7, 3072], P(None, None, 'tensor')
- scale_grad: float32 [3072], P('tensor')
All inputs are finite; a program needn't handle non-finite values.
Results may differ from a plain program's by a relative error of at most 0.022.
Values may be sent and summed in bfloat16 or wider, within the bound.
No kernel may reach another device: no remote copies, remote signals or barrier semaphores. Data moves between devices by JAX's collectives and lax.ppermute only.
A program may use at most 128 MiB of HBM per device.

v0:
```python
import math
import jax
import jax.numpy as jnp
from jax import lax
from jax.sharding import PartitionSpec as P

EPSILON = 1e-06


def extended(cells, sides, width):
    for axis, dim in sides:
        count = lax.axis_size(axis)
        ends = count - 1
        head = lax.slice_in_dim(cells, 0, width, axis=dim)
        tail = lax.slice_in_dim(cells, cells.shape[dim] - width, cells.shape[dim], axis=dim)
        cells = jnp.concatenate(
            [
                lax.ppermute(tail, axis, [(i, (i + 1) % count) for i in range(ends)]),
                cells,
                lax.ppermute(head, axis, [((i + 1) % count, i) for i in range(ends)]),
            ],
            axis=dim,
        )
    return cells


def gelu_exact(values):
    return 0.5 * values * (1.0 + lax.erf(values * (1.0 / math.sqrt(2.0))))


def gelu_slope(values):
    cumulative = 0.5 * (1.0 + lax.erf(values * (1.0 / math.sqrt(2.0))))
    density = jnp.exp(-0.5 * values * values) * (1.0 / math.sqrt(2.0 * math.pi))
    return cumulative + values * density


def depthwise(padded, kernel, height, breadth):
    kernel_size = kernel.shape[0]
    summed = jnp.zeros((height, breadth, kernel.shape[2]), jnp.float32)
    for row_shift in range(kernel_size):
        for col_shift in range(kernel_size):
            window = padded[row_shift : row_shift + height, col_shift : col_shift + breadth]
            summed = summed + kernel[row_shift, col_shift].astype(jnp.float32) * window
    return summed


def kernel_terms(padded, gradient, kernel_size):
    height, breadth = (gradient.shape[0], gradient.shape[1])
    kernel_rows = []
    for row_shift in range(kernel_size):
        kernel_line = []
        for col_shift in range(kernel_size):
            window = padded[row_shift : row_shift + height, col_shift : col_shift + breadth]
            kernel_line.append(jnp.sum(window * gradient, axis=(0, 1)))
        kernel_rows.append(jnp.stack(kernel_line))
    return jnp.stack(kernel_rows)


def contract_last(left, right):
    return lax.dot_general(
        left, right, (((1,), (1,)), ((), ())), preferred_element_type=jnp.float32
    )


def contract_first(left, right):
    return lax.dot_general(
        left, right, (((0,), (0,)), ((), ())), preferred_element_type=jnp.float32
    )


def per_device(
    image,
    dw_kernel,
    dw_bias,
    norm_gain,
    norm_bias,
    w_expand,
    b_expand,
    w_project,
    b_project,
    layer_scale,
    out_grad,
):
    kernel_size = dw_kernel.shape[0]
    rim_depth = kernel_size // 2
    height, breadth, channels = image.shape
    positions = height * breadth
    features = norm_gain.shape[0]
    channel_start = lax.axis_index("tensor") * channels
    gain_part = lax.dynamic_slice_in_dim(norm_gain, channel_start, channels)
    shift_part = lax.dynamic_slice_in_dim(norm_bias, channel_start, channels)
    rimmed = extended(image, (("rows", 0),), rim_depth)
    wide_image = jnp.pad(rimmed, ((0, 0), (rim_depth, rim_depth), (0, 0))).astype(jnp.float32)
    convolved = depthwise(wide_image, dw_kernel, height, breadth) + dw_bias
    mixed = convolved.astype(jnp.bfloat16).reshape(positions, channels)
    own_mixed = mixed.astype(jnp.float32)
    plain_sum, square_sum = lax.psum(
        (jnp.sum(own_mixed, 1), jnp.sum(own_mixed * own_mixed, 1)), "tensor"
    )
    average = plain_sum[:, None] / features
    inv_std = lax.rsqrt(square_sum[:, None] / features - average * average + EPSILON)
    centred = (own_mixed - average) * inv_std
    normed_part = (centred * gain_part + shift_part).astype(jnp.bfloat16)
    normed = lax.all_gather(normed_part, "tensor", axis=1, tiled=True)
    columns = normed
    pre = jnp.dot(
        columns,
        lax.all_gather(w_expand, "rows", axis=0, tiled=True),
        preferred_element_type=jnp.float32,
    )
    pre = pre + b_expand
    hidden = gelu_exact(pre).astype(jnp.bfloat16)
    partial_out = jnp.dot(
        hidden,
        lax.all_gather(w_project, "rows", axis=1, tiled=True),
        preferred_element_type=jnp.float32,
    )
    projected = (
        lax.psum_scatter(
            partial_out.astype(jnp.bfloat16), "tensor", scatter_dimension=1, tiled=True
        ).astype(jnp.float32)
        + b_project
    )
    residual = image.reshape(positions, channels).astype(jnp.float32)
    result = (
        (residual + layer_scale * projected).astype(jnp.bfloat16).reshape(height, breadth, channels)
    )
    upstream = out_grad.reshape(positions, channels).astype(jnp.float32)
    scale_term = jnp.sum(upstream * projected, 0)
    scaled_grad = (upstream * layer_scale).astype(jnp.bfloat16)
    grad_panels = lax.all_gather(scaled_grad, "tensor", axis=1, tiled=True)
    project_term = contract_first(hidden, grad_panels)
    project_grad = lax.psum_scatter(
        project_term.astype(jnp.bfloat16), "rows", scatter_dimension=1, tiled=True
    ).astype(jnp.float32)
    columns = grad_panels
    hidden_grad = contract_last(columns, lax.all_gather(w_project, "rows", axis=1, tiled=True))
    pre_grad = (hidden_grad * gelu_slope(pre)).astype(jnp.bfloat16)
    columns = normed
    expand_grad = lax.psum_scatter(
        contract_first(columns, pre_grad).astype(jnp.bfloat16),
        "rows",
        scatter_dimension=0,
        tiled=True,
    ).astype(jnp.float32)
    normed_partial = contract_last(pre_grad, lax.all_gather(w_expand, "rows", axis=0, tiled=True))
    normed_grad = lax.psum_scatter(
        normed_partial.astype(jnp.bfloat16), "tensor", scatter_dimension=1, tiled=True
    ).astype(jnp.float32)
    gain_grad = normed_grad * gain_part
    plain_total, centred_total = lax.psum(
        (jnp.sum(gain_grad, 1), jnp.sum(gain_grad * centred, 1)), "tensor"
    )
    plain_mean = plain_total[:, None] / features
    centred_mean = centred_total[:, None] / features
    mixed_grad = (inv_std * (gain_grad - plain_mean - centred * centred_mean)).astype(jnp.bfloat16)
    mixed_grad = mixed_grad.reshape(height, breadth, channels)
    grad_rimmed = extended(mixed_grad, (("rows", 0),), rim_depth)
    wide_grad = jnp.pad(grad_rimmed, ((0, 0), (rim_depth, rim_depth), (0, 0))).astype(jnp.float32)
    back = depthwise(wide_grad, dw_kernel[::-1, ::-1], height, breadth)
    image_grad = (upstream.reshape(height, breadth, channels) + back).astype(jnp.bfloat16)
    kernel_local = kernel_terms(wide_image, mixed_grad.astype(jnp.float32), kernel_size)
    kernel_grad, scale_grad = lax.psum((kernel_local, scale_term), "rows")
    return (result, image_grad, expand_grad, project_grad, kernel_grad, scale_grad)


def solution(mesh):
    return jax.shard_map(
        per_device,
        mesh=mesh,
        in_specs=(
            P("rows", None, "tensor"),
            P(None, None, "tensor"),
            P("tensor"),
            P(),
            P(),
            P("rows", "tensor"),
            P("tensor"),
            P("tensor", "rows"),
            P("tensor"),
            P("tensor"),
            P("rows", None, "tensor"),
        ),
        out_specs=(
            P("rows", None, "tensor"),
            P("rows", None, "tensor"),
            P("rows", "tensor"),
            P("tensor", "rows"),
            P(None, None, "tensor"),
            P("tensor"),
        ),
        check_vma=False,
    )
```

profile of v0, /device:TPU:38, one launch (start us, length us, event | category | flops | bytes accessed | tf_op | source)
XLA Modules:
  0.0 697.6 jit_solution(9709800327366942939)
XLA Ops:
  8.8 3.5 collective-permute-start
  12.3 4.5 collective-permute-start.1
  16.7 1.0 bitcast_convert_fusion.49
  17.7 1.0 bitcast_convert_fusion.48
  18.7 0.9 bitcast_convert_fusion.47
  21.2 1.0 fusion.106
  22.2 2.7 convert_reduce_fusion
  25.1 65.2 %all-reduce.3 = (f32[512]{0:T(512)S(1)}, f32[512]{0:T(512)S(1)}) all-reduce(f32[512]{0:T(512)S(1)} %reduce_sum.493, f32[512]{0:T(512)S(1)} %reduce_sum.491), channel_id=1, replica_groups=mesh['tensor'=32,'rows'=8] {'tensor'}, use_global_device_ids=true, to_apply=%region_3.4 | all-reduce | flops 1024 | bytes 8192 | tf_op jit(solution)/shard_map/psum | solution.py:97
  91.9 79.8 %all-gather.5.cloned.1.call-done = bf16[512,3072]{0,1:T(8,128)(2,1)} async-done(((bf16[512,96]{0,1:T(8,128)(2,1)}), bf16[512,3072]{0,1:T(8,128)(2,1)}) %all-gather.5.cloned.1.call-update) | async-done | bytes 3145744 | tf_op jit(solution)/shard_map/all_gather | solution.py:104
  171.7 4.5 convolution_add_fusion
  176.2 40.6 %all-gather.9.cloned.1.call-done = bf16[384,3072]{1,0:T(8,128)(2,1)} async-done(((bf16[384,384]{1,0:T(8,128)(2,1)}), bf16[384,3072]{1,0:T(8,128)(2,1)}) %all-gather.9.cloned.1.call-update) | async-done | bytes 2359312 | tf_op jit(solution)/shard_map/all_gather | solution.py:115
  216.8 5.3 convolution_convert_fusion.1
  223.3 120.4 %reduce-scatter.7.cloned.1.call-done = bf16[512,96]{0,1:T(8,128)(2,1)} async-done(((bf16[512,3072]{0,1:T(8,128)(2,1)}), bf16[512,96]{0,1:T(8,128)(2,1)}) %reduce-scatter.7.cloned.1.call-update) | async-done | bytes 98320 | tf_op jit(solution)/shard_map/reduce_scatter | solution.py:119
  343.7 1.8 multiply_reduce_fusion.1
  345.6 82.8 %all-gather.11.cloned.1.call-done = bf16[512,3072]{0,1:T(8,128)(2,1)} async-done(((bf16[512,96]{0,1:T(8,128)(2,1)}), bf16[512,3072]{0,1:T(8,128)(2,1)}) %all-gather.11.cloned.1.call-update) | async-done | bytes 3145744 | tf_op jit(solution)/shard_map/all_gather | solution.py:131
  428.4 4.7 fusion
  433.9 3.5 convolution_convert_fusion
  437.7 3.6 convolution_convert_fusion.2
  441.3 2.5 copy.41
  443.8 5.2 convolution_convert_fusion.3
  449.8 108.2 %reduce-scatter.9.cloned.1.call-done = bf16[512,96]{0,1:T(8,128)(2,1)} async-done(((bf16[512,3072]{0,1:T(8,128)(2,1)}), bf16[512,96]{0,1:T(8,128)(2,1)}) %reduce-scatter.9.cloned.1.call-update) | async-done | bytes 98320 | tf_op jit(solution)/shard_map/reduce_scatter | solution.py:147
  557.9 1.0 fusion.108
  558.9 60.7 %all-reduce.2 = (f32[512]{0:T(512)S(1)}, f32[512]{0:T(512)S(1)}) all-reduce(f32[512]{0:T(512)S(1)} %get-tuple-element.64, f32[512]{0:T(512)S(1)} %get-tuple-element.63), channel_id=1, replica_groups=mesh['tensor'=32,'rows'=8] {'tensor'}, use_global_device_ids=true, to_apply=%region_9.10 | all-reduce | flops 1024 | bytes 8192 | tf_op jit(solution)/shard_map/psum | solution.py:151
  619.7 1.0 multiply_convert_fusion.1
  621.1 5.2 collective-permute-start.3
  626.3 1.9 collective-permute-start.2
  630.3 1.2 copy.42
  631.4 0.9 convert_element_type.306
  632.3 22.2 %reduce-scatter.11.cloned.1.call-done = bf16[384,384]{1,0:T(8,128)(2,1)} async-done(((bf16[3072,384]{1,0:T(8,128)(2,1)}), bf16[384,384]{1,0:T(8,128)(2,1)}) %reduce-scatter.11.cloned.1.call-update) | async-done | bytes 294928 | tf_op jit(solution)/shard_map/reduce_scatter | solution.py:140
  654.5 1.8 convert_element_type.304
  656.3 32.2 %all-reduce.4 = (f32[7,7,96]{2,1,0:T(8,128)}, f32[96]{0:T(128)}) all-reduce(f32[7,7,96]{2,1,0:T(8,128)S(1)} %constant_dynamic-update-slice_fusion, f32[96]{0:T(128)S(1)} %get-tuple-element.72), channel_id=1, replica_groups=mesh['tensor'=32,'rows'=8] {'rows'}, use_global_device_ids=true, to_apply=%region_61.62 | all-reduce | flops 4800 | bytes 38400 | tf_op jit(solution)/shard_map/psum | solution.py:163
  688.6 2.2 fusion.57
  (73 shorter events, 10.4 us)
Async XLA Ops:
  7.2 84.7 %all-gather.7.cloned.1.call-start = ((), (), s32[]{:S(2)}) async-start(), calls=%async_computation.5 | async-start | bytes 2654208 | tf_op jit(solution)/shard_map/all_gather | solution.py:108
  7.9 163.8 %all-gather.5.cloned.1.call-start = ((), (), s32[]{:S(2)}) async-start(), calls=%async_computation.4 | async-start | bytes 3244032 | tf_op jit(solution)/shard_map/all_gather | solution.py:104
  8.8 12.4 %collective-permute-start = (bf16[3,64,96]{2,1,0:T(8,128)(2,1)S(1)}, bf16[3,64,96]{2,1,0:T(8,128)(2,1)S(1)}, u32[]{:S(2)}, u32[]{:S(2)}) collective-permute-start(bf16[3,64,96]{2,1,0:T(8,128)(2,1)S(1)} %get-tuple-element.74), channel_id=1, source_target_pairs={{0,1},{1,2},{2,3},{3,4},{4,5},{5,6},{6,7},{8,9},{9,10},{10,11},{11... | collective-permute-start | bytes 110600 | tf_op jit(solution)/shard_map/ppermute | solution.py:18
  12.3 8.9 %collective-permute-start.1 = (bf16[3,64,96]{2,1,0:T(8,128)(2,1)S(1)}, bf16[3,64,96]{2,1,0:T(8,128)(2,1)S(1)}, u32[]{:S(2)}, u32[]{:S(2)}) collective-permute-start(bf16[3,64,96]{2,1,0:T(8,128)(2,1)S(1)} %get-tuple-element.75), channel_id=1, source_target_pairs={{1,0},{2,1},{3,2},{4,3},{5,4},{6,5},{7,6},{9,8},{10,9},{11,10},{12... | collective-permute-start | bytes 110600 | tf_op jit(solution)/shard_map/ppermute | solution.py:20
  22.2 149.6 %copy-start.5 = (f32[384]{0:T(512)S(1)}, f32[384]{0:T(512)}, u32[]{:S(2)}) copy-start(f32[384]{0:T(512)} %param.17) | copy-start | bytes 4612
  91.1 125.7 %all-gather.9.cloned.1.call-start = ((), (), s32[]{:S(2)}) async-start(), calls=%async_computation.6 | async-start | bytes 2654208 | tf_op jit(solution)/shard_map/all_gather | solution.py:115
  91.8 251.9 %reduce-scatter.7.cloned.1.call-start = ((), (), s32[]{:S(2)}) async-start(), calls=%async_computation.7 | async-start | bytes 3244032 | tf_op jit(solution)/shard_map/reduce_scatter | solution.py:119
  176.2 40.7 %copy-start.6 = (f32[512,384]{1,0:T(8,128)}, f32[512,384]{1,0:T(8,128)S(1)}, u32[]{:S(2)}) copy-start(f32[512,384]{1,0:T(8,128)S(1)} %convolution_add_fusion) | copy-start | bytes 2359300
  222.1 0.9 copy-start.1
  222.1 1.0 copy-start
  222.1 121.6 %copy-start.2 = (f32[96]{0:T(128)S(1)}, f32[96]{0:T(128)}, u32[]{:S(2)}) copy-start(f32[96]{0:T(128)} %param.19) | copy-start | bytes 1156
  222.1 121.6 %copy-start.3 = (f32[96]{0:T(128)S(1)}, f32[96]{0:T(128)}, u32[]{:S(2)}) copy-start(f32[96]{0:T(128)} %param.20) | copy-start | bytes 1156
  222.1 206.2 %all-gather.11.cloned.1.call-start = ((), (), s32[]{:S(2)}) async-start(), calls=%async_computation.8 | async-start | bytes 3244032 | tf_op jit(solution)/shard_map/all_gather | solution.py:131
  345.5 88.4 %copy-start.4 = (bf16[3072,384]{1,0:T(8,128)(2,1)S(1)}, bf16[3072,384]{1,0:T(8,128)(2,1)}, u32[]{:S(2)}) copy-start(bf16[3072,384]{1,0:T(8,128)(2,1)} %all-gather.7.cloned.1.call-done) | copy-start | bytes 7077892
  345.5 212.4 %reduce-scatter.9.cloned.1.call-start = ((), (), s32[]{:S(2)}) async-start(), calls=%async_computation.9 | async-start | bytes 3244032 | tf_op jit(solution)/shard_map/reduce_scatter | solution.py:147
  433.1 0.7 copy-start.7
  437.4 192.8 %reduce-scatter.13.cloned.1.call-start = ((), (), s32[]{:S(2)}) async-start(), calls=%async_computation.11 | async-start | bytes 2654208
  443.7 210.7 %reduce-scatter.11.cloned.1.call-start = ((), (), s32[]{:S(2)}) async-start(), calls=%async_computation.10 | async-start | bytes 2654208 | tf_op jit(solution)/shard_map/reduce_scatter | solution.py:140
  621.1 67.4 %collective-permute-start.3 = (bf16[3,64,96]{2,1,0:T(8,128)(2,1)S(1)}, bf16[3,64,96]{2,1,0:T(8,128)(2,1)S(1)}, u32[]{:S(2)}, u32[]{:S(2)}) collective-permute-start(bf16[3,64,96]{2,1,0:T(8,128)(2,1)S(1)} %bitcast.289), channel_id=1, source_target_pairs={{1,0},{2,1},{3,2},{4,3},{5,4},{6,5},{7,6},{9,8},{10,9},{11,10},{12... | collective-permute-start | bytes 110600 | tf_op jit(solution)/shard_map/ppermute | solution.py:20
  626.3 62.2 %collective-permute-start.2 = (bf16[3,64,96]{2,1,0:T(8,128)(2,1)S(1)}, bf16[3,64,96]{2,1,0:T(8,128)(2,1)S(1)}, u32[]{:S(2)}, u32[]{:S(2)}) collective-permute-start(bf16[3,64,96]{2,1,0:T(8,128)(2,1)S(1)} %bitcast.288), channel_id=1, source_target_pairs={{0,1},{1,2},{2,3},{3,4},{4,5},{5,6},{6,7},{8,9},{9,10},{10,11},{11... | collective-permute-start | bytes 110600 | tf_op jit(solution)/shard_map/ppermute | solution.py:18
Sparse Core Ops, SparseCore 0:
  9.8 46.1 all-gather.6
  91.2 80.4 all-gather.4
  173.5 43.2 all-gather.8
  222.3 121.3 reduce-scatter.6
  347.3 81.0 all-gather.10
  437.5 120.3 reduce-scatter.8
  560.5 45.4 reduce-scatter.12
  608.6 45.8 reduce-scatter.10
where the time goes:
time: 698 us
  waiting for transfers between devices  456 us (65%)
  blocking collectives  158 us (23%)
  matrix products  26.7 us (4%)
  other arithmetic  17.7 us (3%)
  starting transfers between devices  15.6 us (2%)
  between operations  14.4 us (2%)
  local copies, waits for them, and re-layouts  9.46 us (1%)
    reduce_scatter x1, waiting for transfers between devices, per_device(): lax.psum_scatter(partial_out.astype(jnp.bfloat16), 'tensor', scatter_dime...  120 us
    reduce_scatter x1, waiting for transfers between devices, per_device(): lax.psum_scatter(normed_partial.astype(jnp.bfloat16), 'tensor', scatter_d...  108 us
    all_gather x1, waiting for transfers between devices, per_device(): grad_panels = lax.all_gather(scaled_grad, 'tensor', axis=1, tiled=True)  82.8 us
    all_gather x1, waiting for transfers between devices, per_device(): normed = lax.all_gather(normed_part, 'tensor', axis=1, tiled=True)  79.8 us
    psum x1, blocking collectives, per_device(): lax.psum((jnp.sum(own_mixed, 1), jnp.sum(own_mixed * own_mixed, 1)), 'ten...  65.2 us
    psum x1, blocking collectives, per_device(): lax.psum((jnp.sum(gain_grad, 1), jnp.sum(gain_grad * centred, 1)), 'tensor')  60.7 us
    all_gather x1, waiting for transfers between devices, per_device(): lax.all_gather(w_project, 'rows', axis=1, tiled=True)  40.6 us
    psum x1, blocking collectives, per_device(): kernel_grad, scale_grad = lax.psum((kernel_local, scale_term), 'rows')  32.2 us
  transfers between devices with their start and end apart: 12, of which 6 were waited for; matrix products, arithmetic and copies ran while one was open for 5% of the time, Pallas kernels for 0%

commit v1 on v0

--- a/solution.py
+++ b/solution.py
@@ -1,10 +1,24 @@
+import functools
 import math
 import jax
 import jax.numpy as jnp
 from jax import lax
 from jax.sharding import PartitionSpec as P
+from jax.lax import all_to_all, axis_size
 
 EPSILON = 1e-06
+
+
+def assign_the_knots(vals, peer_axis):
+    shelf = []
+    for _ in range(axis_size(peer_axis)):
+        shelf.append(vals)
+    return jnp.concatenate(
+        all_to_all(jnp.stack(shelf), peer_axis, split_axis=0, concat_axis=0), axis=1
+    )
+
+
+_store_desk = functools.partial(assign_the_knots, peer_axis="tensor")
 
 
 def extended(cells, sides, width):
@@ -101,7 +115,7 @@
     inv_std = lax.rsqrt(square_sum[:, None] / features - average * average + EPSILON)
     centred = (own_mixed - average) * inv_std
     normed_part = (centred * gain_part + shift_part).astype(jnp.bfloat16)
-    normed = lax.all_gather(normed_part, "tensor", axis=1, tiled=True)
+    normed = _store_desk(normed_part)
     columns = normed
     pre = jnp.dot(
         columns,

time: 698 us -> 661 us (0.947)
  waiting for transfers between devices: 456 us -> 404 us
  starting transfers between devices: 15.6 us -> 27.5 us
    all_gather x1 -> x0, waiting for transfers between devices: 79.8 us -> none  [per_device(): normed = lax.all_gather(normed_part, 'tensor', axis=1, tiled=True)]
    all_to_all x0 -> x1, waiting for transfers between devices: none -> 69.4 us  [assign_the_knots(): all_to_all(jnp.stack(shelf), peer_axis, split_axis=0, concat_axis=0)]
    all_gather x1, waiting for transfers between devices: 40.6 us -> 0.02 us  [per_device(): lax.all_gather(w_project, 'rows', axis=1, tiled=True)]
    all_to_all x0 -> x1, starting transfers between devices: none -> 12.1 us  [assign_the_knots(): all_to_all(jnp.stack(shelf), peer_axis, split_axis=0, concat_axis=0)]
  transfers between devices with their start and end apart: 12 -> 12, of which waited for: 6 -> 5; matrix products, arithmetic and copies ran while one was open for 5% -> 5% of each run, Pallas kernels for 0% -> 0%
where the time goes in v1:
time: 661 us; the launch traced here: 660 us
  waiting for transfers between devices  404 us (61%)
  blocking collectives  159 us (24%)
  starting transfers between devices  27.5 us (4%)
  matrix products  26.8 us (4%)
  other arithmetic  17 us (3%)
  between operations  14.4 us (2%)
  local copies, waits for them, and re-layouts  12.4 us (2%)
    reduce_scatter x1, waiting for transfers between devices, per_device(): lax.psum_scatter(partial_out.astype(jnp.bfloat16), 'tensor', scatter_dime...  120 us
    reduce_scatter x1, waiting for transfers between devices, per_device(): lax.psum_scatter(normed_partial.astype(jnp.bfloat16), 'tensor', scatter_d...  108 us
    all_gather x1, waiting for transfers between devices, per_device(): grad_panels = lax.all_gather(scaled_grad, 'tensor', axis=1, tiled=True)  82.7 us
    all_to_all x1, waiting for transfers between devices, assign_the_knots(): all_to_all(jnp.stack(shelf), peer_axis, split_axis=0, concat_axis=0)  69.4 us
    psum x1, blocking collectives, per_device(): lax.psum((jnp.sum(own_mixed, 1), jnp.sum(own_mixed * own_mixed, 1)), 'ten...  65.2 us
    psum x1, blocking collectives, per_device(): lax.psum((jnp.sum(gain_grad, 1), jnp.sum(gain_grad * centred, 1)), 'tensor')  60.7 us
    psum x1, blocking collectives, per_device(): kernel_grad, scale_grad = lax.psum((kernel_local, scale_term), 'rows')  32.6 us
    reduce_scatter x1, waiting for transfers between devices, per_device(): lax.psum_scatter(contract_first(columns, pre_grad).astype(jnp.bfloat16),...  21.7 us
  transfers between devices with their start and end apart: 12, of which 5 were waited for; matrix products, arithmetic and copies ran while one was open for 5% of the time, Pallas kernels for 0%

profile of v1, /device:TPU:38, one launch (start us, length us, event | category | flops | bytes accessed | tf_op | source)
XLA Modules:
  0.0 660.3 jit_solution(5477954143671447938)
XLA Ops:
  8.7 3.5 collective-permute-start
  12.2 4.5 collective-permute-start.1
  16.7 1.0 bitcast_convert_fusion.49
  17.7 1.0 bitcast_convert_fusion.48
  21.1 1.0 fusion.106
  22.1 2.6 convert_reduce_fusion
  25.0 65.2 %all-reduce.3 = (f32[512]{0:T(512)S(1)}, f32[512]{0:T(512)S(1)}) all-reduce(f32[512]{0:T(512)S(1)} %reduce_sum.493, f32[512]{0:T(512)S(1)} %reduce_sum.491), channel_id=1, replica_groups=mesh['tensor'=32,'rows'=8] {'tensor'}, use_global_device_ids=true, to_apply=%region_3.4 | all-reduce | flops 1024 | bytes 8192 | tf_op jit(solution)/shard_map/psum | solution.py:111
  90.4 2.1 stack.227
  92.4 12.1 %all-to-all-start = ((bf16[32,512,96]{1,2,0:T(8,128)(2,1)}), bf16[32,512,96]{1,2,0:T(8,128)(2,1)}, u32[]{:S(2)}, u32[]{:S(2)}) async-start(bf16[32,512,96]{1,2,0:T(8,128)(2,1)} %stack.227), calls=%async_computation | async-start | bytes 6291456 | tf_op jit(solution)/shard_map/all_to_all | solution.py:17
  105.3 69.4 %all-to-all-done = bf16[32,512,96]{1,2,0:T(8,128)(2,1)} async-done(((bf16[32,512,96]{1,2,0:T(8,128)(2,1)}), bf16[32,512,96]{1,2,0:T(8,128)(2,1)}, u32[]{:S(2)}, u32[]{:S(2)}) %all-to-all-start) | async-done | bytes 3145760 | tf_op jit(solution)/shard_map/all_to_all | solution.py:17
  174.8 4.5 convolution_add_fusion
  179.3 0.9 copy-done.6
  180.2 5.3 convolution_convert_fusion.1
  186.6 120.2 %reduce-scatter.7.cloned.1.call-done = bf16[512,96]{0,1:T(8,128)(2,1)} async-done(((bf16[512,3072]{0,1:T(8,128)(2,1)}), bf16[512,96]{0,1:T(8,128)(2,1)}) %reduce-scatter.7.cloned.1.call-update) | async-done | bytes 98320 | tf_op jit(solution)/shard_map/reduce_scatter | solution.py:133
  306.8 1.8 multiply_reduce_fusion.1
  308.7 82.7 %all-gather.8.cloned.1.call-done = bf16[512,3072]{0,1:T(8,128)(2,1)} async-done(((bf16[512,96]{0,1:T(8,128)(2,1)}), bf16[512,3072]{0,1:T(8,128)(2,1)}) %all-gather.8.cloned.1.call-update) | async-done | bytes 3145744 | tf_op jit(solution)/shard_map/all_gather | solution.py:145
  391.4 4.7 fusion
  396.9 3.6 convolution_convert_fusion
  400.7 3.6 convolution_convert_fusion.2
  404.3 2.5 copy.42
  406.8 5.2 convolution_convert_fusion.3
  412.8 108.1 %reduce-scatter.9.cloned.1.call-done = bf16[512,96]{0,1:T(8,128)(2,1)} async-done(((bf16[512,3072]{0,1:T(8,128)(2,1)}), bf16[512,96]{0,1:T(8,128)(2,1)}) %reduce-scatter.9.cloned.1.call-update) | async-done | bytes 98320 | tf_op jit(solution)/shard_map/reduce_scatter | solution.py:161
  520.9 1.0 fusion.108
  521.9 60.7 %all-reduce.2 = (f32[512]{0:T(512)S(1)}, f32[512]{0:T(512)S(1)}) all-reduce(f32[512]{0:T(512)S(1)} %get-tuple-element.64, f32[512]{0:T(512)S(1)} %get-tuple-element.63), channel_id=1, replica_groups=mesh['tensor'=32,'rows'=8] {'tensor'}, use_global_device_ids=true, to_apply=%region_9.10 | all-reduce | flops 1024 | bytes 8192 | tf_op jit(solution)/shard_map/psum | solution.py:165
  582.7 1.0 multiply_convert_fusion.1
  584.1 5.1 collective-permute-start.3
  589.2 1.9 collective-permute-start.2
  593.2 1.2 copy.43
  595.2 21.7 %reduce-scatter.11.cloned.1.call-done = bf16[384,384]{1,0:T(8,128)(2,1)} async-done(((bf16[3072,384]{1,0:T(8,128)(2,1)}), bf16[384,384]{1,0:T(8,128)(2,1)}) %reduce-scatter.11.cloned.1.call-update) | async-done | bytes 294928 | tf_op jit(solution)/shard_map/reduce_scatter | solution.py:154
  616.9 1.8 convert_element_type.308
  618.7 32.6 %all-reduce.4 = (f32[7,7,96]{2,1,0:T(8,128)}, f32[96]{0:T(128)}) all-reduce(f32[7,7,96]{2,1,0:T(8,128)S(1)} %constant_dynamic-update-slice_fusion, f32[96]{0:T(128)S(1)} %get-tuple-element.72), channel_id=1, replica_groups=mesh['tensor'=32,'rows'=8] {'rows'}, use_global_device_ids=true, to_apply=%region_61.62 | all-reduce | flops 4800 | bytes 38400 | tf_op jit(solution)/shard_map/psum | solution.py:177
  651.3 2.2 fusion.57
  (73 shorter events, 11.5 us)
Async XLA Ops:
  7.2 98.2 %all-gather.4.cloned.1.call-start = ((), (), s32[]{:S(2)}) async-start(), calls=%async_computation.5 | async-start | bytes 2654208 | tf_op jit(solution)/shard_map/all_gather | solution.py:122
  8.7 12.4 %collective-permute-start = (bf16[3,64,96]{2,1,0:T(8,128)(2,1)S(1)}, bf16[3,64,96]{2,1,0:T(8,128)(2,1)S(1)}, u32[]{:S(2)}, u32[]{:S(2)}) collective-permute-start(bf16[3,64,96]{2,1,0:T(8,128)(2,1)S(1)} %get-tuple-element.74), channel_id=1, source_target_pairs={{0,1},{1,2},{2,3},{3,4},{4,5},{5,6},{6,7},{8,9},{9,10},{10,11},{11... | collective-permute-start | bytes 110600 | tf_op jit(solution)/shard_map/ppermute | solution.py:32
  12.2 8.9 %collective-permute-start.1 = (bf16[3,64,96]{2,1,0:T(8,128)(2,1)S(1)}, bf16[3,64,96]{2,1,0:T(8,128)(2,1)S(1)}, u32[]{:S(2)}, u32[]{:S(2)}) collective-permute-start(bf16[3,64,96]{2,1,0:T(8,128)(2,1)S(1)} %get-tuple-element.75), channel_id=1, source_target_pairs={{1,0},{2,1},{3,2},{4,3},{5,4},{6,5},{7,6},{9,8},{10,9},{11,10},{12... | collective-permute-start | bytes 110600 | tf_op jit(solution)/shard_map/ppermute | solution.py:34
  92.4 82.3 %copy-start.5 = (f32[384]{0:T(512)S(1)}, f32[384]{0:T(512)}, u32[]{:S(2)}) copy-start(f32[384]{0:T(512)} %param.17) | copy-start | bytes 4612
  92.4 82.3 %all-to-all-start = ((bf16[32,512,96]{1,2,0:T(8,128)(2,1)}), bf16[32,512,96]{1,2,0:T(8,128)(2,1)}, u32[]{:S(2)}, u32[]{:S(2)}) async-start(bf16[32,512,96]{1,2,0:T(8,128)(2,1)} %stack.227), calls=%async_computation | async-start | bytes 6291456 | tf_op jit(solution)/shard_map/all_to_all | solution.py:17
  104.5 74.8 %all-gather.6.cloned.1.call-start = ((), (), s32[]{:S(2)}) async-start(), calls=%async_computation.6 | async-start | bytes 2654208 | tf_op jit(solution)/shard_map/all_gather | solution.py:129
  105.3 201.6 %reduce-scatter.7.cloned.1.call-start = ((), (), s32[]{:S(2)}) async-start(), calls=%async_computation.7 | async-start | bytes 3244032 | tf_op jit(solution)/shard_map/reduce_scatter | solution.py:133
  179.2 0.9 copy-start.6
  185.4 0.9 copy-start.1
  185.4 1.0 copy-start
  185.4 121.4 %copy-start.2 = (f32[96]{0:T(128)S(1)}, f32[96]{0:T(128)}, u32[]{:S(2)}) copy-start(f32[96]{0:T(128)} %param.19) | copy-start | bytes 1156
  185.4 121.4 %copy-start.3 = (f32[96]{0:T(128)S(1)}, f32[96]{0:T(128)}, u32[]{:S(2)}) copy-start(f32[96]{0:T(128)} %param.20) | copy-start | bytes 1156
  185.5 205.9 %all-gather.8.cloned.1.call-start = ((), (), s32[]{:S(2)}) async-start(), calls=%async_computation.8 | async-start | bytes 3244032 | tf_op jit(solution)/shard_map/all_gather | solution.py:145
  308.6 88.3 %copy-start.4 = (bf16[3072,384]{1,0:T(8,128)(2,1)S(1)}, bf16[3072,384]{1,0:T(8,128)(2,1)}, u32[]{:S(2)}) copy-start(bf16[3072,384]{1,0:T(8,128)(2,1)} %all-gather.4.cloned.1.call-done) | copy-start | bytes 7077892
  308.6 212.3 %reduce-scatter.9.cloned.1.call-start = ((), (), s32[]{:S(2)}) async-start(), calls=%async_computation.9 | async-start | bytes 3244032 | tf_op jit(solution)/shard_map/reduce_scatter | solution.py:161
  396.1 0.7 copy-start.7
  400.4 192.7 %reduce-scatter.13.cloned.1.call-start = ((), (), s32[]{:S(2)}) async-start(), calls=%async_computation.11 | async-start | bytes 2654208
  406.8 210.1 %reduce-scatter.11.cloned.1.call-start = ((), (), s32[]{:S(2)}) async-start(), calls=%async_computation.10 | async-start | bytes 2654208 | tf_op jit(solution)/shard_map/reduce_scatter | solution.py:154
  584.1 67.1 %collective-permute-start.3 = (bf16[3,64,96]{2,1,0:T(8,128)(2,1)S(1)}, bf16[3,64,96]{2,1,0:T(8,128)(2,1)S(1)}, u32[]{:S(2)}, u32[]{:S(2)}) collective-permute-start(bf16[3,64,96]{2,1,0:T(8,128)(2,1)S(1)} %bitcast.292), channel_id=1, source_target_pairs={{1,0},{2,1},{3,2},{4,3},{5,4},{6,5},{7,6},{9,8},{10,9},{11,10},{12... | collective-permute-start | bytes 110600 | tf_op jit(solution)/shard_map/ppermute | solution.py:34
  589.2 62.0 %collective-permute-start.2 = (bf16[3,64,96]{2,1,0:T(8,128)(2,1)S(1)}, bf16[3,64,96]{2,1,0:T(8,128)(2,1)S(1)}, u32[]{:S(2)}, u32[]{:S(2)}) collective-permute-start(bf16[3,64,96]{2,1,0:T(8,128)(2,1)S(1)} %bitcast.291), channel_id=1, source_target_pairs={{0,1},{1,2},{2,3},{3,4},{4,5},{5,6},{6,7},{8,9},{9,10},{10,11},{11... | collective-permute-start | bytes 110600 | tf_op jit(solution)/shard_map/ppermute | solution.py:32
Sparse Core Ops, SparseCore 0:
  9.8 46.1 all-gather.3
  107.1 58.6 all-gather.5
  185.6 121.1 reduce-scatter.6
  310.4 80.9 all-gather.7
  400.6 120.3 reduce-scatter.8
  523.4 45.4 reduce-scatter.12
  571.4 45.3 reduce-scatter.10
